TPU v7x, 32 devices: a whole 2x2x4 slice. The times are simulated.
32 devices in a mesh: dp: 4 (over z), pipe: 2 (over core), expert: 4 (over y, x).
Axes of the slice: x: 2, y: 2, z: 4, core: 2. Of those that a mesh axis runs over, the one named last changes fastest.
Arguments:
- tokens: bfloat16 [2, 96, 3072], P(None, 'expert'), may hold values from -6 to 6
- expert_ids: int32 [2, 2, 96, 2], P('pipe', None, 'expert'), may hold values from 0 to 3, all different within a row; in each aligned block of 24 rows (0 to 23, 24 to 47, ..., all dimensions but the last counted through in order) at most 16 rows name the same one
- gates: float32 [2, 2, 96, 2], P('pipe', None, 'expert'), may hold values from 0.1 to 1
- w_gate: bfloat16 [2, 4, 3072, 704], P('pipe', 'expert', None, 'dp'), may hold values from -0.109375 to 0.109375
- w_up: bfloat16 [2, 4, 3072, 704], P('pipe', 'expert', None, 'dp'), may hold values from -0.109375 to 0.109375
- w_down: bfloat16 [2, 4, 704, 3072], P('pipe', 'expert', 'dp'), may hold values from -0.3125 to 0.3125
Outputs:
- layer_out: bfloat16 [2, 2, 96, 3072], P('pipe', None, 'expert', 'dp')
Inputs may be any that keep to these rules, and one draw needn't show every extreme that they name: `expert_ids`: each token names 2 different experts in each layer. Among the tokens of one index of expert in one layer and micro-batch (aligned blocks of 24 tokens) no expert is named by more than 16 tokens, and in some block an expert is named by exactly 16.
All inputs are finite; a program needn't handle non-finite values.
Results may differ from a plain program's by a relative error of at most 0.0052.
Values may be sent and summed in bfloat16 or wider, within the bound.
No kernel may reach another device: no remote copies, remote signals or barrier semaphores. Data moves between devices by JAX's collectives and lax.ppermute only.
A program may use at most 64 MiB of HBM per device.

v0:
```python
import jax
import jax.numpy as jnp
from jax import lax
from jax.sharding import PartitionSpec as P

TOP = 2
CAP = 16


def passed_along(value, axis, by):
    length = lax.axis_size(axis)
    pairs = [(i, i + by) for i in range(length) if 0 <= i + by < length]
    return lax.ppermute(value, axis, pairs)


def build_maps(route_ids, route_gates, experts, rows_all):
    flat_ids = route_ids.reshape(-1)
    onehot = (flat_ids[:, None] == jnp.arange(experts, dtype=jnp.int32)[None, :]).astype(jnp.int32)
    before = jnp.cumsum(onehot, axis=0) - onehot
    placed = flat_ids * CAP + jnp.sum(before * onehot, axis=1)
    matches = jnp.arange(rows_all, dtype=jnp.int32)[:, None] == placed[None, :]
    dispatch_map = jnp.sum(matches.astype(jnp.float32).reshape(rows_all, -1, TOP), axis=2).astype(
        jnp.bfloat16
    )
    combine_map = jnp.sum(
        jnp.where(matches, route_gates.reshape(-1)[None, :], 0.0).reshape(rows_all, -1, TOP), axis=2
    )
    return (dispatch_map, combine_map)


def per_device(tokens, expert_ids, gates, w_gate, w_up, w_down):
    experts = lax.axis_size("expert")
    dp_size = lax.axis_size("dp")
    sections = lax.axis_size("pipe")
    micro_count = tokens.shape[0]
    tok_rows = tokens.shape[1]
    model_width = tokens.shape[2]
    unit_count = w_gate.shape[3]
    columns = model_width // dp_size
    rows_all = experts * CAP
    gate_local = w_gate[0, 0]
    up_local = w_up[0, 0]
    down_local = w_down[0, 0]
    section = lax.axis_index("pipe")
    is_first = section == 0
    column_start = lax.axis_index("dp") * columns
    outputs = jnp.zeros((1, micro_count, tok_rows, columns), jnp.bfloat16)
    carried = jnp.zeros((tok_rows, model_width), jnp.bfloat16)
    turns = micro_count + sections - 1
    for moment in range(turns):
        offset_micro = moment - section
        in_window = (offset_micro >= 0) & (offset_micro < micro_count)
        micro_index = jnp.clip(offset_micro, 0, micro_count - 1)
        own_rows = tokens[min(moment, micro_count - 1)]
        route_ids = lax.dynamic_index_in_dim(expert_ids[0], micro_index, 0, keepdims=False)
        route_gates = lax.dynamic_index_in_dim(gates[0], micro_index, 0, keepdims=False)
        dispatch_map, combine_map = build_maps(route_ids, route_gates, experts, rows_all)
        current = jnp.where(is_first, own_rows, carried)
        current_cols = lax.dynamic_slice_in_dim(current, column_start, columns, 1)
        outgoing = jnp.dot(dispatch_map, current, preferred_element_type=jnp.float32)
        outgoing = outgoing.astype(jnp.bfloat16).reshape(experts, CAP, model_width)
        arrived = lax.all_to_all(outgoing, "expert", split_axis=0, concat_axis=0, tiled=True)
        flat_rows = arrived.reshape(-1, model_width)
        squares = jnp.mean(jnp.square(flat_rows.astype(jnp.float32)), axis=1, keepdims=True)
        inv_rms = lax.rsqrt(squares + 1e-05)
        gate_act = jnp.dot(flat_rows, gate_local, preferred_element_type=jnp.float32) * inv_rms
        up_act = jnp.dot(flat_rows, up_local, preferred_element_type=jnp.float32) * inv_rms
        hidden_rows = (jax.nn.silu(gate_act) * up_act).astype(jnp.bfloat16)
        hidden = hidden_rows.reshape(arrived.shape[0], arrived.shape[1], unit_count)
        hidden = hidden.reshape(rows_all, unit_count)
        summed = lax.psum_scatter(
            lax.dot_general(
                down_local, hidden, (((0,), (1,)), ((), ())), preferred_element_type=jnp.float32
            ),
            "dp",
            scatter_dimension=0,
            tiled=True,
        )
        shares = summed.astype(jnp.bfloat16).reshape(columns, experts, CAP)
        returned = lax.all_to_all(
            shares, "expert", split_axis=1, concat_axis=1, tiled=True
        ).reshape(columns, rows_all)
        mixed = lax.dot_general(
            combine_map,
            returned.astype(jnp.float32),
            (((0,), (1,)), ((), ())),
            precision=lax.Precision.HIGHEST,
            preferred_element_type=jnp.float32,
        )
        new_cols = (current_cols.astype(jnp.float32) + mixed).astype(jnp.bfloat16)
        updated = lax.dynamic_update_slice_in_dim(outputs, new_cols[None, None], micro_index, 1)
        outputs = jnp.where(in_window, updated, outputs)
        if moment + 1 < turns:
            full_rows = lax.all_gather(new_cols, "dp", axis=1, tiled=True)
            carried = passed_along(full_rows, "pipe", 1)
    return outputs


def solution(mesh):
    return jax.shard_map(
        per_device,
        mesh=mesh,
        in_specs=(
            P(None, "expert", None),
            P("pipe", None, "expert", None),
            P("pipe", None, "expert", None),
            P("pipe", "expert", None, "dp"),
            P("pipe", "expert", None, "dp"),
            P("pipe", "expert", "dp", None),
        ),
        out_specs=P("pipe", None, "expert", "dp"),
        check_vma=False,
    )
```

profile of v0, /device:TPU:0, one launch (start us, length us, event | category | flops | bytes accessed | tf_op | source)
XLA Modules:
  0.0 198.9 jit_solution(14078611586446322383)
XLA Ops:
  8.9 0.9 slice_select_fusion
  10.1 12.1 %all_to_all.30 = bf16[4,16,3072]{2,1,0:T(8,128)(2,1)S(1)} all-to-all(bf16[4,16,3072]{2,1,0:T(8,128)(2,1)S(1)} %bitcast.104), channel_id=1, replica_groups=mesh['dp'=4,'pipe'=2,'expert'=4] {'expert'}, dimensions={0} | all-to-all | bytes 786432 | tf_op jit(solution)/shard_map/all_to_all | solution.py:62
  23.2 1.5 convolution_multiply_fusion.5
  24.8 2.8 %convolution_bitcast_fusion.2 = f32[3072,64]{0,1:T(8,128)} fusion(bf16[64,3072]{1,0:T(8,128)(2,1)} %bitcast.99, bf16[1,1,176,3072]{3,2,1,0:T(8,128)(2,1)S(1)} %copy-done, bf16[1,1,3072,176]{2,3,1,0:T(8,128)(2,1)S(1)} %copy-done.2, f32[64,176]{1,0:T(8,128)S(1)} %convolution_multiply_fusion.5, f32[64]{0:T(128)S(1)} %rsqrt.34), kind=kOutput, calls=%fused_computation.2 | convolution fusion | flops 138490880 | bytes 3387648 | tf_op jit(solution)/shard_map/dot_general | solution.py:72
  28.7 22.1 %reduce-scatter.4.cloned.1.call-done = f32[768,64]{0,1:T(8,128)} async-done(((f32[3072,64]{0,1:T(8,128)}), f32[768,64]{0,1:T(8,128)}) %reduce-scatter.4.cloned.1.call-update) | async-done | bytes 196624 | tf_op jit(solution)/shard_map/reduce_scatter | solution.py:71
  50.8 1.6 convert_element_type.101
  52.4 3.6 %all-to-all-start.1 = ((bf16[768,4,16]{0,2,1:T(8,128)(2,1)}), bf16[768,4,16]{0,2,1:T(8,128)(2,1)S(1)}, u32[]{:S(2)}, u32[]{:S(2)}) async-start(bf16[768,4,16]{0,2,1:T(8,128)(2,1)} %bitcast.110), calls=%async_computation.2 | async-start | bytes 196608 | tf_op jit(solution)/shard_map/all_to_all | solution.py:80
  56.4 4.6 %all-to-all-done.1 = bf16[768,4,16]{0,2,1:T(8,128)(2,1)S(1)} async-done(((bf16[768,4,16]{0,2,1:T(8,128)(2,1)}), bf16[768,4,16]{0,2,1:T(8,128)(2,1)S(1)}, u32[]{:S(2)}, u32[]{:S(2)}) %all-to-all-start.1) | async-done | bytes 98336 | tf_op jit(solution)/shard_map/all_to_all | solution.py:80
  61.2 13.5 %all_gather.6 = bf16[24,3072]{1,0:T(8,128)(2,1)S(1)} all-gather(bf16[24,768]{1,0:T(8,128)(2,1)S(1)} %get-tuple-element.20), channel_id=1, replica_groups=mesh['dp'=4,'pipe'=2,'expert'=4] {'dp'}, dimensions={1}, use_global_device_ids=true | all-gather | bytes 184320 | tf_op jit(solution)/shard_map/all_gather | solution.py:94
  74.6 1.3 collective-permute-start
  76.0 0.9 collective-permute-done
  76.9 0.9 bitcast_select_fusion.1
  78.1 10.3 %all_to_all.31 = bf16[4,16,3072]{2,1,0:T(8,128)(2,1)S(1)} all-to-all(bf16[4,16,3072]{2,1,0:T(8,128)(2,1)S(1)} %bitcast.105), channel_id=1, replica_groups=mesh['dp'=4,'pipe'=2,'expert'=4] {'expert'}, dimensions={0} | all-to-all | bytes 786432 | tf_op jit(solution)/shard_map/all_to_all | solution.py:62
  89.5 1.5 convolution_multiply_fusion.3
  90.9 2.8 %convolution_bitcast_fusion.1 = f32[3072,64]{0,1:T(8,128)} fusion(bf16[64,3072]{1,0:T(8,128)(2,1)} %bitcast.101, bf16[1,1,176,3072]{3,2,1,0:T(8,128)(2,1)S(1)} %copy-done, bf16[1,1,3072,176]{2,3,1,0:T(8,128)(2,1)S(1)} %copy-done.2, f32[64,176]{1,0:T(8,128)S(1)} %convolution_multiply_fusion.3, f32[64]{0:T(128)S(1)} %rsqrt.36), kind=kOutput, calls=%fused_computation.1 | convolution fusion | flops 138490880 | bytes 3387648 | tf_op jit(solution)/shard_map/dot_general | solution.py:72
  93.8 21.2 %reduce-scatter.6.cloned.1.call-done = f32[768,64]{0,1:T(8,128)} async-done(((f32[3072,64]{0,1:T(8,128)}), f32[768,64]{0,1:T(8,128)}) %reduce-scatter.6.cloned.1.call-update) | async-done | bytes 196624 | tf_op jit(solution)/shard_map/reduce_scatter | solution.py:71
  115.1 1.6 convert_element_type.110
  116.6 3.7 %all-to-all-start.3 = ((bf16[768,4,16]{0,2,1:T(8,128)(2,1)}), bf16[768,4,16]{0,2,1:T(8,128)(2,1)S(1)}, u32[]{:S(2)}, u32[]{:S(2)}) async-start(bf16[768,4,16]{0,2,1:T(8,128)(2,1)} %bitcast.111), calls=%async_computation.5 | async-start | bytes 196608 | tf_op jit(solution)/shard_map/all_to_all | solution.py:80
  120.3 4.9 %all-to-all-done.3 = bf16[768,4,16]{0,2,1:T(8,128)(2,1)S(1)} async-done(((bf16[768,4,16]{0,2,1:T(8,128)(2,1)}), bf16[768,4,16]{0,2,1:T(8,128)(2,1)S(1)}, u32[]{:S(2)}, u32[]{:S(2)}) %all-to-all-start.3) | async-done | bytes 98336 | tf_op jit(solution)/shard_map/all_to_all | solution.py:80
  125.2 1.6 fusion.38
  126.8 13.4 %all_gather.7 = bf16[24,3072]{1,0:T(8,128)(2,1)S(1)} all-gather(bf16[24,768]{1,0:T(8,128)(2,1)S(1)} %get-tuple-element.12), channel_id=1, replica_groups=mesh['dp'=4,'pipe'=2,'expert'=4] {'dp'}, dimensions={1}, use_global_device_ids=true | all-gather | bytes 184320 | tf_op jit(solution)/shard_map/all_gather | solution.py:94
  140.2 1.3 collective-permute-start.1
  141.5 0.9 collective-permute-done.1
  142.4 0.9 bitcast_select_fusion
  143.7 10.3 %all_to_all.32 = bf16[4,16,3072]{2,1,0:T(8,128)(2,1)S(1)} all-to-all(bf16[4,16,3072]{2,1,0:T(8,128)(2,1)S(1)} %bitcast.106), channel_id=1, replica_groups=mesh['dp'=4,'pipe'=2,'expert'=4] {'expert'}, dimensions={0} | all-to-all | bytes 786432 | tf_op jit(solution)/shard_map/all_to_all | solution.py:62
  155.0 1.5 convolution_multiply_fusion.1
  156.5 2.9 %convolution_bitcast_fusion = f32[3072,64]{0,1:T(8,128)} fusion(bf16[64,3072]{1,0:T(8,128)(2,1)} %bitcast.103, bf16[1,1,176,3072]{3,2,1,0:T(8,128)(2,1)S(1)} %copy-done, bf16[1,1,3072,176]{2,3,1,0:T(8,128)(2,1)S(1)} %copy-done.2, f32[64,176]{1,0:T(8,128)S(1)} %convolution_multiply_fusion.1, f32[64]{0:T(128)S(1)} %rsqrt.38), kind=kOutput, calls=%fused_computation | convolution fusion | flops 138490880 | bytes 3387648 | tf_op jit(solution)/shard_map/dot_general | solution.py:72
  159.3 21.3 %reduce-scatter.8.cloned.1.call-done = f32[768,64]{0,1:T(8,128)} async-done(((f32[3072,64]{0,1:T(8,128)}), f32[768,64]{0,1:T(8,128)}) %reduce-scatter.8.cloned.1.call-update) | async-done | bytes 196624 | tf_op jit(solution)/shard_map/reduce_scatter | solution.py:71
  180.7 1.6 convert_element_type.119
  182.2 3.7 %all-to-all-start.5 = ((bf16[768,4,16]{0,2,1:T(8,128)(2,1)}), bf16[768,4,16]{0,2,1:T(8,128)(2,1)S(1)}, u32[]{:S(2)}, u32[]{:S(2)}) async-start(bf16[768,4,16]{0,2,1:T(8,128)(2,1)} %bitcast.27), calls=%async_computation.8 | async-start | bytes 196608 | tf_op jit(solution)/shard_map/all_to_all | solution.py:80
  185.9 4.9 %all-to-all-done.5 = bf16[768,4,16]{0,2,1:T(8,128)(2,1)S(1)} async-done(((bf16[768,4,16]{0,2,1:T(8,128)(2,1)}), bf16[768,4,16]{0,2,1:T(8,128)(2,1)S(1)}, u32[]{:S(2)}, u32[]{:S(2)}) %all-to-all-start.5) | async-done | bytes 98336 | tf_op jit(solution)/shard_map/all_to_all | solution.py:80
  190.8 1.6 fusion.37
  (62 shorter events, 7.9 us)
Async XLA Ops:
  6.5 18.2 %copy-start = (bf16[1,1,176,3072]{3,2,1,0:T(8,128)(2,1)S(1)}, bf16[1,1,176,3072]{3,2,1,0:T(8,128)(2,1)}, u32[]{:S(2)}) copy-start(bf16[1,1,176,3072]{3,2,1,0:T(8,128)(2,1)} %param.11) | copy-start | bytes 3244036
  6.5 44.3 %reduce-scatter.4.cloned.1.call-start = ((), (), s32[]{:S(2)}) async-start(), calls=%async_computation.9 | async-start | bytes 983040 | tf_op jit(solution)/shard_map/reduce_scatter | solution.py:71
  7.6 15.6 %copy-start.1 = (bf16[1,1,3072,176]{2,3,1,0:T(8,128)(2,1)S(1)}, bf16[1,1,3072,176]{2,3,1,0:T(8,128)(2,1)}, u32[]{:S(2)}) copy-start(bf16[1,1,3072,176]{2,3,1,0:T(8,128)(2,1)} %param.9) | copy-start | bytes 3244036
  22.2 0.7 copy-start.3
  23.0 1.8 copy-start.2
  52.4 8.6 %all-to-all-start.1 = ((bf16[768,4,16]{0,2,1:T(8,128)(2,1)}), bf16[768,4,16]{0,2,1:T(8,128)(2,1)S(1)}, u32[]{:S(2)}, u32[]{:S(2)}) async-start(bf16[768,4,16]{0,2,1:T(8,128)(2,1)} %bitcast.110), calls=%async_computation.2 | async-start | bytes 196608 | tf_op jit(solution)/shard_map/all_to_all | solution.py:80
  56.0 59.0 %reduce-scatter.6.cloned.1.call-start = ((), (), s32[]{:S(2)}) async-start(), calls=%async_computation.10 | async-start | bytes 983040 | tf_op jit(solution)/shard_map/reduce_scatter | solution.py:71
  61.2 16.7 %copy-start.6 = (bf16[1,2,24,768]{3,2,1,0:T(8,128)(2,1)}, bf16[1,2,24,768]{3,2,1,0:T(8,128)(2,1)S(1)}, u32[]{:S(2)}) copy-start(bf16[1,2,24,768]{3,2,1,0:T(8,128)(2,1)S(1)} %get-tuple-element.19) | copy-start | bytes 221188
  74.6 2.3 %collective-permute-start = (bf16[24,3072]{1,0:T(8,128)(2,1)S(1)}, bf16[24,3072]{1,0:T(8,128)(2,1)S(1)}, u32[]{:S(2)}, u32[]{:S(2)}) collective-permute-start(bf16[24,3072]{1,0:T(8,128)(2,1)S(1)} %all_gather.6), channel_id=1, source_target_pairs={{0,4},{1,5},{2,6},{3,7},{8,12},{9,13},{10,14},{11,15},{16,20},{17,... | collective-permute-start | bytes 442376 | tf_op jit(solution)/shard_map/ppermute | solution.py:13
  88.5 0.7 copy-start.4
  116.6 8.6 %all-to-all-start.3 = ((bf16[768,4,16]{0,2,1:T(8,128)(2,1)}), bf16[768,4,16]{0,2,1:T(8,128)(2,1)S(1)}, u32[]{:S(2)}, u32[]{:S(2)}) async-start(bf16[768,4,16]{0,2,1:T(8,128)(2,1)} %bitcast.111), calls=%async_computation.5 | async-start | bytes 196608 | tf_op jit(solution)/shard_map/all_to_all | solution.py:80
  120.3 60.4 %reduce-scatter.8.cloned.1.call-start = ((), (), s32[]{:S(2)}) async-start(), calls=%async_computation.11 | async-start | bytes 983040 | tf_op jit(solution)/shard_map/reduce_scatter | solution.py:71
  140.2 2.3 %collective-permute-start.1 = (bf16[24,3072]{1,0:T(8,128)(2,1)S(1)}, bf16[24,3072]{1,0:T(8,128)(2,1)S(1)}, u32[]{:S(2)}, u32[]{:S(2)}) collective-permute-start(bf16[24,3072]{1,0:T(8,128)(2,1)S(1)} %all_gather.7), channel_id=1, source_target_pairs={{0,4},{1,5},{2,6},{3,7},{8,12},{9,13},{10,14},{11,15},{16,20},{17,... | collective-permute-start | bytes 442376 | tf_op jit(solution)/shard_map/ppermute | solution.py:13
  154.0 0.7 copy-start.5
  182.2 8.6 %all-to-all-start.5 = ((bf16[768,4,16]{0,2,1:T(8,128)(2,1)}), bf16[768,4,16]{0,2,1:T(8,128)(2,1)S(1)}, u32[]{:S(2)}, u32[]{:S(2)}) async-start(bf16[768,4,16]{0,2,1:T(8,128)(2,1)} %bitcast.27), calls=%async_computation.8 | async-start | bytes 196608 | tf_op jit(solution)/shard_map/all_to_all | solution.py:80
Sparse Core Ops, SparseCore 0:
  27.8 23.0 reduce-scatter.3
  93.9 21.0 reduce-scatter.5
  159.5 21.1 reduce-scatter.7
where the time goes:
time: 200 us; the launch traced here: 199 us
  waiting for transfers between devices  81 us (40%)
  blocking collectives  59.6 us (30%)
  matrix products  17.2 us (9%)
  starting transfers between devices  13.5 us (7%)
  between operations  13.3 us (7%)
  other arithmetic  9.16 us (5%)
  local copies, waits for them, and re-layouts  5.17 us (3%)
    reduce_scatter x3, waiting for transfers between devices, per_device(): lax.psum_scatter(lax.dot_general(down_local, hidden, (((0,), (1,)), ((),...  64.7 us
    all_to_all x3, blocking collectives, per_device(): lax.all_to_all(outgoing, 'expert', split_axis=0, concat_axis=0, tiled=True)  32.7 us
    all_gather x2, blocking collectives, per_device(): full_rows = lax.all_gather(new_cols, 'dp', axis=1, tiled=True)  26.9 us
    all_to_all x3, waiting for transfers between devices, per_device(): lax.all_to_all(shares, 'expert', split_axis=1, concat_axis=1, tiled=True)  14.4 us
    all_to_all x3, starting transfers between devices, per_device(): lax.all_to_all(shares, 'expert', split_axis=1, concat_axis=1, tiled=True)  11 us
    dot_general x3, matrix products, per_device(): lax.dot_general(down_local, hidden, (((0,), (1,)), ((), ())), preferred_e...  8.54 us
    convert_element_type x3, other arithmetic, per_device(): shares = summed.astype(jnp.bfloat16).reshape(columns, experts, CAP)  4.68 us
    dot_general x3, matrix products, per_device(): jnp.dot(flat_rows, gate_local, preferred_element_type=jnp.float32) * inv_rms  4.54 us
  transfers between devices with their start and end apart: 8, of which 8 were waited for; matrix products, arithmetic and copies ran while one was open for 1% of the time, Pallas kernels for 0%

commit v1 on v0

--- a/solution.py
+++ b/solution.py
@@ -5,6 +5,27 @@
 
 TOP = 2
 CAP = 16
+
+
+def ring_gather(x, axis, dim):
+    size, index, width = (lax.axis_size(axis), lax.axis_index(axis), x.shape[dim])
+    right = [(i, (i + 1) % size) for i in range(size)]
+    behind = [(i, (i - 1) % size) for i in range(size)]
+    out = jnp.zeros((*x.shape[:dim], size * width, *x.shape[dim + 1 :]), x.dtype)
+    out = lax.dynamic_update_slice_in_dim(out, x, index * width, axis=dim)
+    from_left = from_right = x
+    middle = size // 2
+    for lap in range(1, middle + 1):
+        from_left = lax.ppermute(from_left, axis, right)
+        out = lax.dynamic_update_slice_in_dim(
+            out, from_left, (index - lap) % size * width, axis=dim
+        )
+        if lap < size - middle:
+            from_right = lax.ppermute(from_right, axis, behind)
+            out = lax.dynamic_update_slice_in_dim(
+                out, from_right, (index + lap) % size * width, axis=dim
+            )
+    return out
 
 
 def passed_along(value, axis, by):
@@ -91,7 +112,7 @@
         updated = lax.dynamic_update_slice_in_dim(outputs, new_cols[None, None], micro_index, 1)
         outputs = jnp.where(in_window, updated, outputs)
         if moment + 1 < turns:
-            full_rows = lax.all_gather(new_cols, "dp", axis=1, tiled=True)
+            full_rows = ring_gather(new_cols, "dp", 1)
             carried = passed_along(full_rows, "pipe", 1)
     return outputs
 

time: 200 us -> 191 us (0.955)
  blocking collectives: 59.6 us -> 41.1 us
  waiting for transfers between devices: 81 us -> 88.8 us
  starting transfers between devices: 13.5 us -> 17.8 us
    all_gather x2 -> x0, blocking collectives: 26.9 us -> none  [per_device(): full_rows = lax.all_gather(new_cols, 'dp', axis=1, tiled=True)]
    ppermute x0 -> x6, waiting for transfers between devices: none -> 15.3 us  [the longest x4 15.3 us: ring_gather(): from_left = lax.ppermute(from_left, axis, right)]
    all_to_all x0 -> x1, blocking collectives: none -> 8.4 us  [per_device(): lax.all_to_all(shares, 'expert', split_axis=1, concat_axis=1, tiled=True)]
    ppermute x0 -> x6, starting transfers between devices: none -> 7.74 us  [the longest x2 7.62 us: ring_gather(): from_right = lax.ppermute(from_right, axis, behind)]
    all_to_all x3 -> x2, waiting for transfers between devices: 14.4 us -> 9.47 us  [per_device(): lax.all_to_all(shares, 'expert', split_axis=1, concat_axis=1, tiled=True)]
    all_to_all x3 -> x2, starting transfers between devices: 11 us -> 7.44 us  [per_device(): lax.all_to_all(shares, 'expert', split_axis=1, concat_axis=1, tiled=True)]
    reduce_scatter x3, waiting for transfers between devices: 64.7 us -> 62.2 us  [per_device(): lax.psum_scatter(lax.dot_general(down_local, hidden, (((0,), (1,)), ((),...]
  transfers between devices with their start and end apart: 8 -> 13, of which waited for: 8 -> 11; matrix products, arithmetic and copies ran while one was open for 1% -> 1% of each run, Pallas kernels for 0% -> 0%
where the time goes in v1:
time: 191 us; the launch traced here: 190 us
  waiting for transfers between devices  88.8 us (46%)
  blocking collectives  41.1 us (22%)
  starting transfers between devices  17.8 us (9%)
  matrix products  15.8 us (8%)
  between operations  13.5 us (7%)
  other arithmetic  7.68 us (4%)
  local copies, waits for them, and re-layouts  5.26 us (3%)
    reduce_scatter x3, waiting for transfers between devices, per_device(): lax.psum_scatter(lax.dot_general(down_local, hidden, (((0,), (1,)), ((),...  62.2 us
    all_to_all x3, blocking collectives, per_device(): lax.all_to_all(outgoing, 'expert', split_axis=0, concat_axis=0, tiled=True)  32.7 us
    ppermute x4, waiting for transfers between devices, ring_gather(): from_left = lax.ppermute(from_left, axis, right)  15.3 us
    all_to_all x2, waiting for transfers between devices, per_device(): lax.all_to_all(shares, 'expert', split_axis=1, concat_axis=1, tiled=True)  9.47 us
    dot_general x3, matrix products, per_device(): lax.dot_general(down_local, hidden, (((0,), (1,)), ((), ())), preferred_e...  8.54 us
    all_to_all x1, blocking collectives, per_device(): lax.all_to_all(shares, 'expert', split_axis=1, concat_axis=1, tiled=True)  8.4 us
    ppermute x2, starting transfers between devices, ring_gather(): from_right = lax.ppermute(from_right, axis, behind)  7.62 us
    all_to_all x2, starting transfers between devices, per_device(): lax.all_to_all(shares, 'expert', split_axis=1, concat_axis=1, tiled=True)  7.44 us
  transfers between devices with their start and end apart: 13, of which 11 were waited for; matrix products, arithmetic and copies ran while one was open for 1% of the time, Pallas kernels for 0%

profile of v1, /device:TPU:0, one launch (start us, length us, event | category | flops | bytes accessed | tf_op | source)
XLA Modules:
  0.0 189.9 jit_solution(10063091718997875540)
XLA Ops:
  8.9 0.9 slice_select_fusion
  10.1 12.1 %all_to_all.30 = bf16[4,16,3072]{2,1,0:T(8,128)(2,1)S(1)} all-to-all(bf16[4,16,3072]{2,1,0:T(8,128)(2,1)S(1)} %bitcast.104), channel_id=1, replica_groups=mesh['dp'=4,'pipe'=2,'expert'=4] {'expert'}, dimensions={0} | all-to-all | bytes 786432 | tf_op jit(solution)/shard_map/all_to_all | solution.py:83
  23.2 1.5 convolution_multiply_fusion.5
  24.8 2.8 %convolution_bitcast_fusion.2 = f32[3072,64]{0,1:T(8,128)} fusion(bf16[64,3072]{1,0:T(8,128)(2,1)} %bitcast.99, bf16[1,1,176,3072]{3,2,1,0:T(8,128)(2,1)S(1)} %copy-done, bf16[1,1,3072,176]{2,3,1,0:T(8,128)(2,1)S(1)} %copy-done.2, f32[64,176]{1,0:T(8,128)S(1)} %convolution_multiply_fusion.5, f32[64]{0:T(128)S(1)} %rsqrt.34), kind=kOutput, calls=%fused_computation.2 | convolution fusion | flops 138490880 | bytes 3387648 | tf_op jit(solution)/shard_map/dot_general | solution.py:93
  28.8 22.1 %reduce-scatter.4.cloned.1.call-done = f32[768,64]{0,1:T(8,128)} async-done(((f32[3072,64]{0,1:T(8,128)}), f32[768,64]{0,1:T(8,128)}) %reduce-scatter.4.cloned.1.call-update) | async-done | bytes 196624 | tf_op jit(solution)/shard_map/reduce_scatter | solution.py:92
  50.8 1.6 convert_element_type.101
  52.4 3.7 %all-to-all-start.1 = ((bf16[768,4,16]{0,2,1:T(8,128)(2,1)}), bf16[768,4,16]{0,2,1:T(8,128)(2,1)S(1)}, u32[]{:S(2)}, u32[]{:S(2)}) async-start(bf16[768,4,16]{0,2,1:T(8,128)(2,1)} %bitcast.110), calls=%async_computation.2 | async-start | bytes 196608 | tf_op jit(solution)/shard_map/all_to_all | solution.py:101
  56.4 4.6 %all-to-all-done.1 = bf16[768,4,16]{0,2,1:T(8,128)(2,1)S(1)} async-done(((bf16[768,4,16]{0,2,1:T(8,128)(2,1)}), bf16[768,4,16]{0,2,1:T(8,128)(2,1)S(1)}, u32[]{:S(2)}, u32[]{:S(2)}) %all-to-all-start.1) | async-done | bytes 98336 | tf_op jit(solution)/shard_map/all_to_all | solution.py:101
  61.3 3.8 %collective-permute-start.1 = (bf16[24,768]{1,0:T(8,128)(2,1)S(1)}, bf16[24,768]{1,0:T(8,128)(2,1)S(1)}, u32[]{:S(2)}, u32[]{:S(2)}) collective-permute-start(bf16[24,768]{1,0:T(8,128)(2,1)S(1)} %get-tuple-element.20), channel_id=1, source_target_pairs={{0,24},{8,0},{16,8},{24,16},{1,25},{9,1},{17,9},{25,17},{2,26},{10... | collective-permute-start | bytes 110600 | tf_op jit(solution)/shard_map/ppermute | solution.py:24
  65.1 1.9 collective-permute-done
  67.1 5.7 %collective-permute-done.2 = bf16[24,768]{1,0:T(8,128)(2,1)S(1)} collective-permute-done((bf16[24,768]{1,0:T(8,128)(2,1)S(1)}, bf16[24,768]{1,0:T(8,128)(2,1)S(1)}, u32[]{:S(2)}, u32[]{:S(2)}) %collective-permute-start.2) | collective-permute-done | bytes 36896 | tf_op jit(solution)/shard_map/ppermute | solution.py:19
  72.8 1.3 collective-permute-start.3
  75.1 0.9 bitcast_select_fusion.1
  76.3 10.3 %all_to_all.31 = bf16[4,16,3072]{2,1,0:T(8,128)(2,1)S(1)} all-to-all(bf16[4,16,3072]{2,1,0:T(8,128)(2,1)S(1)} %bitcast.105), channel_id=1, replica_groups=mesh['dp'=4,'pipe'=2,'expert'=4] {'expert'}, dimensions={0} | all-to-all | bytes 786432 | tf_op jit(solution)/shard_map/all_to_all | solution.py:83
  87.6 1.5 convolution_multiply_fusion.3
  89.1 2.8 %convolution_bitcast_fusion.1 = f32[3072,64]{0,1:T(8,128)} fusion(bf16[64,3072]{1,0:T(8,128)(2,1)} %bitcast.101, bf16[1,1,176,3072]{3,2,1,0:T(8,128)(2,1)S(1)} %copy-done, bf16[1,1,3072,176]{2,3,1,0:T(8,128)(2,1)S(1)} %copy-done.2, f32[64,176]{1,0:T(8,128)S(1)} %convolution_multiply_fusion.3, f32[64]{0:T(128)S(1)} %rsqrt.36), kind=kOutput, calls=%fused_computation.1 | convolution fusion | flops 138490880 | bytes 3387648 | tf_op jit(solution)/shard_map/dot_general | solution.py:93
  92.0 20.1 %reduce-scatter.6.cloned.1.call-done = f32[768,64]{0,1:T(8,128)} async-done(((f32[3072,64]{0,1:T(8,128)}), f32[768,64]{0,1:T(8,128)}) %reduce-scatter.6.cloned.1.call-update) | async-done | bytes 196624 | tf_op jit(solution)/shard_map/reduce_scatter | solution.py:92
  112.1 1.0 convert_element_type.110
  113.1 8.4 %all_to_all.32 = bf16[768,4,16]{0,2,1:T(8,128)(2,1)S(1)} all-to-all(bf16[768,4,16]{0,2,1:T(8,128)(2,1)S(1)} %bitcast.111), channel_id=1, replica_groups=mesh['dp'=4,'pipe'=2,'expert'=4] {'expert'}, dimensions={1} | all-to-all | bytes 196608 | tf_op jit(solution)/shard_map/all_to_all | solution.py:101
  121.7 3.8 %collective-permute-start.5 = (bf16[24,768]{1,0:T(8,128)(2,1)S(1)}, bf16[24,768]{1,0:T(8,128)(2,1)S(1)}, u32[]{:S(2)}, u32[]{:S(2)}) collective-permute-start(bf16[24,768]{1,0:T(8,128)(2,1)S(1)} %get-tuple-element.12), channel_id=1, source_target_pairs={{0,24},{8,0},{16,8},{24,16},{1,25},{9,1},{17,9},{25,17},{2,26},{10... | collective-permute-start | bytes 110600 | tf_op jit(solution)/shard_map/ppermute | solution.py:24
  125.5 1.9 %collective-permute-done.4 = bf16[24,768]{1,0:T(8,128)(2,1)S(1)} collective-permute-done((bf16[24,768]{1,0:T(8,128)(2,1)S(1)}, bf16[24,768]{1,0:T(8,128)(2,1)S(1)}, u32[]{:S(2)}, u32[]{:S(2)}) %collective-permute-start.4) | collective-permute-done | bytes 36896 | tf_op jit(solution)/shard_map/ppermute | solution.py:19
  127.5 5.7 %collective-permute-done.6 = bf16[24,768]{1,0:T(8,128)(2,1)S(1)} collective-permute-done((bf16[24,768]{1,0:T(8,128)(2,1)S(1)}, bf16[24,768]{1,0:T(8,128)(2,1)S(1)}, u32[]{:S(2)}, u32[]{:S(2)}) %collective-permute-start.6) | collective-permute-done | bytes 36896 | tf_op jit(solution)/shard_map/ppermute | solution.py:19
  133.2 1.3 collective-permute-start.7
  134.6 0.9 collective-permute-done.7
  135.8 10.3 %all_to_all.33 = bf16[4,16,3072]{2,1,0:T(8,128)(2,1)S(1)} all-to-all(bf16[4,16,3072]{2,1,0:T(8,128)(2,1)S(1)} %bitcast.106), channel_id=1, replica_groups=mesh['dp'=4,'pipe'=2,'expert'=4] {'expert'}, dimensions={0} | all-to-all | bytes 786432 | tf_op jit(solution)/shard_map/all_to_all | solution.py:83
  147.1 1.5 convolution_multiply_fusion.1
  148.6 2.8 %convolution_bitcast_fusion = f32[3072,64]{0,1:T(8,128)} fusion(bf16[64,3072]{1,0:T(8,128)(2,1)} %bitcast.103, bf16[1,1,176,3072]{3,2,1,0:T(8,128)(2,1)S(1)} %copy-done, bf16[1,1,3072,176]{2,3,1,0:T(8,128)(2,1)S(1)} %copy-done.2, f32[64,176]{1,0:T(8,128)S(1)} %convolution_multiply_fusion.1, f32[64]{0:T(128)S(1)} %rsqrt.38), kind=kOutput, calls=%fused_computation | convolution fusion | flops 138490880 | bytes 3387648 | tf_op jit(solution)/shard_map/dot_general | solution.py:93
  151.5 20.1 %reduce-scatter.8.cloned.1.call-done = f32[768,64]{0,1:T(8,128)} async-done(((f32[3072,64]{0,1:T(8,128)}), f32[768,64]{0,1:T(8,128)}) %reduce-scatter.8.cloned.1.call-update) | async-done | bytes 196624 | tf_op jit(solution)/shard_map/reduce_scatter | solution.py:92
  171.6 1.6 convert_element_type.119
  173.2 3.7 %all-to-all-start.5 = ((bf16[768,4,16]{0,2,1:T(8,128)(2,1)}), bf16[768,4,16]{0,2,1:T(8,128)(2,1)S(1)}, u32[]{:S(2)}, u32[]{:S(2)}) async-start(bf16[768,4,16]{0,2,1:T(8,128)(2,1)} %bitcast.27), calls=%async_computation.8 | async-start | bytes 196608 | tf_op jit(solution)/shard_map/all_to_all | solution.py:101
  176.9 4.9 %all-to-all-done.5 = bf16[768,4,16]{0,2,1:T(8,128)(2,1)S(1)} async-done(((bf16[768,4,16]{0,2,1:T(8,128)(2,1)}), bf16[768,4,16]{0,2,1:T(8,128)(2,1)S(1)}, u32[]{:S(2)}, u32[]{:S(2)}) %all-to-all-start.5) | async-done | bytes 98336 | tf_op jit(solution)/shard_map/all_to_all | solution.py:101
  181.9 1.6 fusion.37
  (87 shorter events, 9.3 us)
Async XLA Ops:
  6.5 18.2 %copy-start = (bf16[1,1,176,3072]{3,2,1,0:T(8,128)(2,1)S(1)}, bf16[1,1,176,3072]{3,2,1,0:T(8,128)(2,1)}, u32[]{:S(2)}) copy-start(bf16[1,1,176,3072]{3,2,1,0:T(8,128)(2,1)} %param.11) | copy-start | bytes 3244036
  6.5 44.3 %reduce-scatter.4.cloned.1.call-start = ((), (), s32[]{:S(2)}) async-start(), calls=%async_computation.9 | async-start | bytes 983040 | tf_op jit(solution)/shard_map/reduce_scatter | solution.py:92
  7.6 15.6 %copy-start.1 = (bf16[1,1,3072,176]{2,3,1,0:T(8,128)(2,1)S(1)}, bf16[1,1,3072,176]{2,3,1,0:T(8,128)(2,1)}, u32[]{:S(2)}) copy-start(bf16[1,1,3072,176]{2,3,1,0:T(8,128)(2,1)} %param.9) | copy-start | bytes 3244036
  22.2 0.7 copy-start.3
  23.0 1.8 copy-start.2
  52.4 8.7 %all-to-all-start.1 = ((bf16[768,4,16]{0,2,1:T(8,128)(2,1)}), bf16[768,4,16]{0,2,1:T(8,128)(2,1)S(1)}, u32[]{:S(2)}, u32[]{:S(2)}) async-start(bf16[768,4,16]{0,2,1:T(8,128)(2,1)} %bitcast.110), calls=%async_computation.2 | async-start | bytes 196608 | tf_op jit(solution)/shard_map/all_to_all | solution.py:101
  56.1 56.0 %reduce-scatter.6.cloned.1.call-start = ((), (), s32[]{:S(2)}) async-start(), calls=%async_computation.10 | async-start | bytes 983040 | tf_op jit(solution)/shard_map/reduce_scatter | solution.py:92
  61.2 14.8 %copy-start.7 = (bf16[1,2,24,768]{3,2,1,0:T(8,128)(2,1)}, bf16[1,2,24,768]{3,2,1,0:T(8,128)(2,1)S(1)}, u32[]{:S(2)}) copy-start(bf16[1,2,24,768]{3,2,1,0:T(8,128)(2,1)S(1)} %get-tuple-element.19) | copy-start | bytes 221188
  61.2 5.8 %collective-permute-start = (bf16[24,768]{1,0:T(8,128)(2,1)S(1)}, bf16[24,768]{1,0:T(8,128)(2,1)S(1)}, u32[]{:S(2)}, u32[]{:S(2)}) collective-permute-start(bf16[24,768]{1,0:T(8,128)(2,1)S(1)} %get-tuple-element.20), channel_id=1, source_target_pairs={{0,8},{8,16},{16,24},{24,0},{1,9},{9,17},{17,25},{25,1},{2,10},{10... | collective-permute-start | bytes 110600 | tf_op jit(solution)/shard_map/ppermute | solution.py:19
  61.3 5.8 %collective-permute-start.1 = (bf16[24,768]{1,0:T(8,128)(2,1)S(1)}, bf16[24,768]{1,0:T(8,128)(2,1)S(1)}, u32[]{:S(2)}, u32[]{:S(2)}) collective-permute-start(bf16[24,768]{1,0:T(8,128)(2,1)S(1)} %get-tuple-element.20), channel_id=1, source_target_pairs={{0,24},{8,0},{16,8},{24,16},{1,25},{9,1},{17,9},{25,17},{2,26},{10... | collective-permute-start | bytes 110600 | tf_op jit(solution)/shard_map/ppermute | solution.py:24
  67.0 5.8 %collective-permute-start.2 = (bf16[24,768]{1,0:T(8,128)(2,1)S(1)}, bf16[24,768]{1,0:T(8,128)(2,1)S(1)}, u32[]{:S(2)}, u32[]{:S(2)}) collective-permute-start(bf16[24,768]{1,0:T(8,128)(2,1)S(1)} %collective-permute-done), channel_id=1, source_target_pairs={{0,8},{8,16},{16,24},{24,0},{1,9},{9,17},{17,25},{25,1},{2,10},{10... | collective-permute-start | bytes 110600 | tf_op jit(solution)/shard_map/ppermute | solution.py:19
  72.8 2.3 %collective-permute-start.3 = (bf16[24,3072]{1,0:T(8,128)(2,1)S(1)}, bf16[24,3072]{1,0:T(8,128)(2,1)S(1)}, u32[]{:S(2)}, u32[]{:S(2)}) collective-permute-start(bf16[24,3072]{1,0:T(8,128)(2,1)S(1)} %constant_dynamic-update-slice_fusion.4), channel_id=1, source_target_pairs={{0,4},{1,5},{2,6},{3,7},{8,12},{9,13},{10,14},{11,15},{16,20},{17,... | collective-permute-start | bytes 442376 | tf_op jit(solution)/shard_map/ppermute | solution.py:34
  86.6 0.7 copy-start.4
  92.0 79.7 %reduce-scatter.8.cloned.1.call-start = ((), (), s32[]{:S(2)}) async-start(), calls=%async_computation.11 | async-start | bytes 983040 | tf_op jit(solution)/shard_map/reduce_scatter | solution.py:92
  112.1 23.4 %copy-start.6 = (bf16[2,24,3072]{2,1,0:T(8,128)(2,1)S(1)}, bf16[2,24,3072]{2,1,0:T(8,128)(2,1)}, u32[]{:S(2)}) copy-start(bf16[2,24,3072]{2,1,0:T(8,128)(2,1)} %param.6) | copy-start | bytes 884740
  121.7 5.8 %collective-permute-start.4 = (bf16[24,768]{1,0:T(8,128)(2,1)S(1)}, bf16[24,768]{1,0:T(8,128)(2,1)S(1)}, u32[]{:S(2)}, u32[]{:S(2)}) collective-permute-start(bf16[24,768]{1,0:T(8,128)(2,1)S(1)} %get-tuple-element.12), channel_id=1, source_target_pairs={{0,8},{8,16},{16,24},{24,0},{1,9},{9,17},{17,25},{25,1},{2,10},{10... | collective-permute-start | bytes 110600 | tf_op jit(solution)/shard_map/ppermute | solution.py:19
  121.7 5.8 %collective-permute-start.5 = (bf16[24,768]{1,0:T(8,128)(2,1)S(1)}, bf16[24,768]{1,0:T(8,128)(2,1)S(1)}, u32[]{:S(2)}, u32[]{:S(2)}) collective-permute-start(bf16[24,768]{1,0:T(8,128)(2,1)S(1)} %get-tuple-element.12), channel_id=1, source_target_pairs={{0,24},{8,0},{16,8},{24,16},{1,25},{9,1},{17,9},{25,17},{2,26},{10... | collective-permute-start | bytes 110600 | tf_op jit(solution)/shard_map/ppermute | solution.py:24
  127.5 5.8 %collective-permute-start.6 = (bf16[24,768]{1,0:T(8,128)(2,1)S(1)}, bf16[24,768]{1,0:T(8,128)(2,1)S(1)}, u32[]{:S(2)}, u32[]{:S(2)}) collective-permute-start(bf16[24,768]{1,0:T(8,128)(2,1)S(1)} %collective-permute-done.4), channel_id=1, source_target_pairs={{0,8},{8,16},{16,24},{24,0},{1,9},{9,17},{17,25},{25,1},{2,10},{10... | collective-permute-start | bytes 110600 | tf_op jit(solution)/shard_map/ppermute | solution.py:19
  133.2 2.3 %collective-permute-start.7 = (bf16[24,3072]{1,0:T(8,128)(2,1)S(1)}, bf16[24,3072]{1,0:T(8,128)(2,1)S(1)}, u32[]{:S(2)}, u32[]{:S(2)}) collective-permute-start(bf16[24,3072]{1,0:T(8,128)(2,1)S(1)} %constant_dynamic-update-slice_fusion), channel_id=1, source_target_pairs={{0,4},{1,5},{2,6},{3,7},{8,12},{9,13},{10,14},{11,15},{16,20},{17,... | collective-permute-start | bytes 442376 | tf_op jit(solution)/shard_map/ppermute | solution.py:34
  146.2 0.7 copy-start.5
  151.5 25.4 %copy-start.8 = (bf16[1,2,24,768]{3,2,1,0:T(8,128)(2,1)S(1)}, bf16[1,2,24,768]{3,2,1,0:T(8,128)(2,1)}, u32[]{:S(2)}) copy-start(bf16[1,2,24,768]{3,2,1,0:T(8,128)(2,1)} %copy-done.7) | copy-start | bytes 221188
  173.2 8.7 %all-to-all-start.5 = ((bf16[768,4,16]{0,2,1:T(8,128)(2,1)}), bf16[768,4,16]{0,2,1:T(8,128)(2,1)S(1)}, u32[]{:S(2)}, u32[]{:S(2)}) async-start(bf16[768,4,16]{0,2,1:T(8,128)(2,1)} %bitcast.27), calls=%async_computation.8 | async-start | bytes 196608 | tf_op jit(solution)/shard_map/all_to_all | solution.py:101
  176.9 4.9 %copy-start.9 = (bf16[1,2,24,768]{3,2,1,0:T(8,128)(2,1)}, bf16[1,2,24,768]{3,2,1,0:T(8,128)(2,1)S(1)}, u32[]{:S(2)}) copy-start(bf16[1,2,24,768]{3,2,1,0:T(8,128)(2,1)S(1)} %fusion.38) | copy-start | bytes 221188
Sparse Core Ops, SparseCore 0:
  27.8 23.0 reduce-scatter.3
  92.1 19.9 reduce-scatter.5
  151.6 19.9 reduce-scatter.7
